TPU v7x, 256 devices: a whole 4x4x8 slice. The times are simulated.
256 devices in a mesh: dp: 16 (over z_lo, x), tensor: 16 (over y, z_hi, core).
Axes of the slice: x: 4, y: 4, z: 8 (z_hi: 2, z_lo: 4; z = z_hi * 4 + z_lo), core: 2. Of those that a mesh axis runs over, the one named last changes fastest.
Arguments:
- inner_x: bfloat16 [16, 2048, 7168], P('dp', None, 'tensor')
- gate_z: bfloat16 [16, 2048, 7168], P('dp', None, 'tensor'), may hold values from -6 to 6
- input_b: bfloat16 [16, 2048, 128], P('dp'), may hold values from -0.75 to 0.75
- output_c: bfloat16 [16, 2048, 128], P('dp'), may hold values from -6 to 6
- step_raw: float32 [16, 2048, 112], P('dp', None, 'tensor'), may hold values from -6 to 6
- decay_rate: float32 [112], P('tensor'), may hold values from 0.001 to 0.05
- skip_gain: float32 [112], P('tensor'), may hold values from 0.5 to 1.5
- norm_gain: float32 [7168], P('tensor'), may hold values from 0.5 to 1.5
- out_weight: bfloat16 [7168, 3584], P('tensor'), may hold values from -0.0625 to 0.0625
- segment: int32 [16, 2048], P('dp'), may hold values from 0 to 7, never falling along the last dimension, each value on 1 to 1024 neighbouring positions
- cache_slot: int32 [16, 8], replicated, may hold values from 0 to 127, as said below
Outputs:
- mixed: bfloat16 [16, 2048, 3584], P('dp', 'tensor')
- cache: float32 [128, 112, 4096], P('dp', 'tensor')
Inputs may be any that keep to these rules, and one draw needn't show every extreme that they name: `segment`: in each group's row the prompt numbers never fall and every prompt 0 to 7 is present. `cache_slot`: every slot is named exactly once; slot // 8 is the owning group, and no two prompts of one group have the same owning group.
All inputs are finite; a program needn't handle non-finite values.
Results may differ from a plain program's by a relative error of at most 0.018.
Values may be sent and summed in bfloat16 or wider, within the bound.
No kernel may reach another device: no remote copies, remote signals or barrier semaphores. Data moves between devices by JAX's collectives and lax.ppermute only.
A program may use at most 192 MiB of HBM per device.

v0:
```python
import jax
import jax.numpy as jnp
from jax import lax
from jax.sharding import PartitionSpec as P

HEADS = 112
HEAD = 64
STATE = 64
NGROUPS = 2
REQS = 8
BLOCK = 256
INNER = 7168
HIGHEST = lax.Precision.HIGHEST


def split_pair(values):
    upper = values.astype(jnp.bfloat16)
    lower = (values - upper.astype(jnp.float32)).astype(jnp.bfloat16)
    return (upper, lower)


def split_einsum(form, wide, narrow):
    upper, lower = split_pair(wide)
    first = jnp.einsum(form, upper, narrow, preferred_element_type=jnp.float32)
    return first + jnp.einsum(form, lower, narrow, preferred_element_type=jnp.float32)


def local(
    inner_x,
    gate_z,
    input_b,
    output_c,
    step_raw,
    decay_rate,
    skip_gain,
    norm_gain,
    out_weight,
    segment,
    cache_slot,
):
    stream_len = inner_x.shape[1]
    dev_width = inner_x.shape[2]
    dev_heads = decay_rate.shape[0]
    tensor_idx = lax.axis_index("tensor")
    group_idx = tensor_idx * dev_heads // (HEADS // NGROUPS)
    b_cols = lax.dynamic_slice_in_dim(input_b[0], group_idx * STATE, STATE, 1)
    c_cols = lax.dynamic_slice_in_dim(output_c[0], group_idx * STATE, STATE, 1)
    step_size = jax.nn.softplus(step_raw[0])
    cum_log = jnp.cumsum(-decay_rate[None, :] * step_size, axis=0)
    seg_row = segment[0]
    block_count = stream_len // BLOCK
    x_blk = inner_x[0].reshape(block_count, BLOCK, dev_heads, HEAD)
    cum_blk = cum_log.reshape(block_count, BLOCK, dev_heads)
    step_blk = step_size.reshape(block_count, BLOCK, dev_heads)
    seg_blk = seg_row.reshape(block_count, BLOCK)
    b_blk = b_cols.reshape(block_count, BLOCK, STATE)
    c_blk = c_cols.reshape(block_count, BLOCK, STATE)
    positions = jnp.arange(BLOCK)
    scores = jnp.einsum("btn,bsn->bts", c_blk, b_blk, preferred_element_type=jnp.float32)
    causal_mask = (positions[None, None, :] <= positions[None, :, None]) & (
        seg_blk[:, :, None] == seg_blk[:, None, :]
    )
    cum_t = cum_blk.transpose(0, 2, 1)
    log_gap = cum_t[:, :, :, None] - cum_t[:, :, None, :]
    weights = (
        jnp.exp(jnp.where(causal_mask[:, None], log_gap, -jnp.inf))
        * step_blk.transpose(0, 2, 1)[:, :, None, :]
        * scores[:, None]
    )
    intra_part = split_einsum("bhts,bshp->bthp", weights, x_blk)
    last_seg = seg_blk[:, -1]
    last_cum = cum_blk[:, -1]
    pull_back = (
        jnp.exp(last_cum[:, None, :] - cum_blk)
        * step_blk
        * (seg_blk == last_seg[:, None]).astype(jnp.float32)[:, :, None]
    )
    added = split_einsum("bshp,bsn->bhpn", pull_back[:, :, :, None] * x_blk, b_blk)
    prev_cum = jnp.concatenate([jnp.zeros((1, dev_heads), jnp.float32), last_cum[:-1]], axis=0)
    prev_seg = jnp.concatenate([jnp.full((1,), -1, seg_row.dtype), last_seg[:-1]], axis=0)
    blocks = jnp.arange(block_count)
    earlier = blocks[None, :] < blocks[:, None]
    mix_ok = earlier & (last_seg[None, :] == prev_seg[:, None])
    mix_gap = prev_cum[:, None, :] - last_cum[None, :, :]
    mix = jnp.exp(jnp.where(mix_ok[:, :, None], mix_gap, -jnp.inf))
    carried = jnp.sum(mix[:, :, :, None, None] * added[None], axis=1)
    live_rows = (seg_blk == prev_seg[:, None]).astype(jnp.float32)
    carry_decay = jnp.exp(cum_blk - prev_cum[:, None, :]) * live_rows[:, :, None]
    carry_part = split_einsum("bhpn,btn->bthp", carried, c_blk) * carry_decay[:, :, :, None]
    outputs = intra_part + carry_part + skip_gain[None, None, :, None] * x_blk.astype(jnp.float32)
    mixer_y = outputs.reshape(stream_len, dev_width)
    members = (seg_row[None, :] == jnp.arange(REQS)[:, None]).astype(jnp.float32)
    end_index = (
        jnp.sum((seg_row[None, :] <= jnp.arange(REQS)[:, None]).astype(jnp.int32), axis=1) - 1
    )
    at_end = (jnp.arange(stream_len)[None, :] == end_index[:, None]).astype(jnp.float32)
    end_cum = jnp.dot(at_end, cum_log, precision=HIGHEST)
    seg_end_cum = jnp.dot(members.T, end_cum, precision=HIGHEST)
    pull_all = jnp.exp(seg_end_cum - cum_log) * step_size
    weighted = (inner_x[0].reshape(stream_len, dev_heads, HEAD) * pull_all[:, :, None]).reshape(
        stream_len, dev_width
    )
    masked_b = (
        (members.astype(jnp.bfloat16)[:, :, None] * b_cols[None])
        .transpose(1, 0, 2)
        .reshape(stream_len, REQS * STATE)
    )
    finals = split_einsum("tc,tk->ck", weighted, masked_b)
    finals = (
        finals.reshape(dev_heads, HEAD, REQS, STATE)
        .transpose(2, 0, 1, 3)
        .reshape(REQS, dev_heads * HEAD * STATE)
    )
    gated = mixer_y * jax.nn.silu(gate_z[0].astype(jnp.float32))
    sum_sq = jnp.sum(gated * gated, axis=1)
    group_hot = (jnp.arange(NGROUPS) == group_idx).astype(jnp.float32)
    group_stat = lax.psum(sum_sq[:, None] * group_hot[None, :], "tensor")
    mean_sq = jnp.sum(group_stat * group_hot[None, :], axis=1) / (INNER // NGROUPS)
    rounded = (gated * lax.rsqrt(mean_sq + 1e-05)[:, None] * norm_gain[None, :]).astype(
        jnp.bfloat16
    )
    projected = lax.psum_scatter(
        jnp.dot(rounded, out_weight, preferred_element_type=jnp.float32).astype(jnp.bfloat16),
        "tensor",
        scatter_dimension=0,
        tiled=True,
    )
    mixed = projected[None]
    dp_idx = lax.axis_index("dp")
    dp_size = lax.axis_size("dp")
    own_slots = lax.dynamic_slice_in_dim(cache_slot, dp_idx, 1, 0)[0]
    dest_hot = ((own_slots // REQS)[:, None] == jnp.arange(dp_size)[None, :]).astype(jnp.float32)
    outbound = jnp.dot(dest_hot.T, finals, precision=HIGHEST).reshape(
        dp_size, dev_heads, HEAD * STATE
    )
    inbound = lax.all_to_all(
        outbound.astype(jnp.bfloat16), "dp", split_axis=0, concat_axis=0, tiled=True
    ).astype(outbound.dtype)
    wanted = dp_idx * REQS + jnp.arange(REQS)
    take_hot = jnp.any(cache_slot[:, :, None] == wanted[None, None, :], axis=1).astype(jnp.float32)
    cache = jnp.dot(
        take_hot.T, inbound.reshape(dp_size, dev_heads * HEAD * STATE), precision=HIGHEST
    )
    return (mixed, cache.reshape(REQS, dev_heads, HEAD * STATE))


def solution(mesh):
    in_specs = (
        P("dp", None, "tensor"),
        P("dp", None, "tensor"),
        P("dp", None, None),
        P("dp", None, None),
        P("dp", None, "tensor"),
        P("tensor"),
        P("tensor"),
        P("tensor"),
        P("tensor", None),
        P("dp", None),
        P(),
    )
    out_specs = (P("dp", "tensor", None), P("dp", "tensor", None))
    return jax.shard_map(local, mesh=mesh, in_specs=in_specs, out_specs=out_specs, check_vma=False)
```

profile of v0, /device:TPU:32, one launch (start us, length us, event | category | flops | bytes accessed | tf_op | source)
XLA Modules:
  0.0 360.7 jit_solution(5995153483289453547)
XLA Ops:
  7.2 0.5 broadcast.229
  7.8 1.4 reduce.9
  9.2 0.1 slice.36
  9.3 0.7 neg.22
  10.0 0.9 multiply_bitcast_fusion
  10.9 2.0 reduce-window.6
  12.9 0.2 slice_reduce_fusion
  13.1 0.2 reduce-window.9
  13.2 0.1 add_bitcast_fusion
  13.3 0.6 copy-done.5
  14.0 0.1 slice.37
  14.1 0.1 slice.38
  14.1 0.1 copy.169
  14.2 0.1 copy.168
  14.3 0.9 dynamic-slice_reduce_fusion
  15.2 0.6 and_select_fusion
  15.8 0.7 compare_convert_fusion
  16.5 0.7 fusion.58
  17.1 0.6 copy.241
  17.8 0.6 iota_compare_fusion
  18.4 3.3 copy.177
  21.8 0.1 copy.170
  21.9 0.8 reduce.3
  22.7 0.1 copy.171
  22.8 2.5 constant_dynamic-slice_fusion
  25.3 1.2 copy.167
  26.7 1.0 copy.120
  27.6 1.3 compare_and_fusion
  28.9 1.5 fusion.46
  30.4 0.1 exponential_multiply_fusion
  30.5 5.6 %fusion.4 = f32[8,7,256,64]{2,3,1,0:T(8,128)S(1)} fusion(f32[8,256,256]{2,1,0:T(8,128)S(1)} %fusion.46, f32[8,7,256]{2,1,0:T(8,128)S(1)} %get-tuple-element.6, f32[8,7,256]{2,1,0:T(8,128)S(1)} %copy.120, pred[8,256,256]{2,1,0:T(8,128)(4,1)S(1)} %compare_and_fusion, bf16[8,256,7,64]{1,0,3,2:T(8,128)(2,1)S(1)} %bitcast.162), kind=kOutput, calls=%fused_computation.7 | convolution fusion | flops 488112128 | bytes 8241152 | tf_op jit(solution)/shard_map/bhts,bshp->bthp/dot_general | solution.py:24
  36.1 6.2 %fusion.1 = f32[8,7,256,64]{2,3,1,0:T(8,128)S(1)} fusion(f32[8,256,256]{2,1,0:T(8,128)S(1)} %fusion.46, f32[8,7,256]{2,1,0:T(8,128)S(1)} %get-tuple-element.6, f32[8,7,256]{2,1,0:T(8,128)S(1)} %copy.120, pred[8,256,256]{2,1,0:T(8,128)(4,1)S(1)} %compare_and_fusion, bf16[8,256,7,64]{1,0,3,2:T(8,128)(2,1)S(1)} %bitcast.163), kind=kOutput, calls=%fused_computation.5 | convolution fusion | flops 499122176 | bytes 8241152 | tf_op jit(solution)/shard_map/bhts,bshp->bthp/dot_general | solution.py:25
  42.3 0.4 convert_element_type.188
  42.8 1.7 copy.179
  44.5 0.7 fusion.23
  45.2 0.6 fusion.32
  45.8 0.1 select_exponential_fusion
  45.9 1.8 multiply_reduce_fusion
  47.7 0.6 fusion.44
  48.3 2.8 multiply_reduce_fusion.1
  51.1 2.1 copy.144
  53.2 3.7 %copy.178 = f32[56,8,8,256]{3,1,2,0:T(8,128)} copy(f32[56,8,8,256]{3,2,1,0:T(8,128)S(1)} %bitcast.160) | data formatting | bytes 7340032
  56.9 0.1 broadcast_multiply_fusion.1
  57.0 92.2 %psum.7 = f32[2048,2]{0,1:T(2,128)S(1)} all-reduce(f32[2048,2]{0,1:T(2,128)S(1)} %broadcast_multiply_fusion.1), channel_id=1, replica_groups=mesh['dp'=16,'tensor'=16] {'tensor'}, use_global_device_ids=true, to_apply=%region_4.5 | all-reduce | flops 4096 | bytes 32768 | tf_op jit(solution)/shard_map/psum | solution.py:117
  149.2 0.1 multiply_reduce_fusion.2
  149.3 15.2 %convolution_convert_fusion = bf16[2048,3584]{1,0:T(8,128)(2,1)} fusion(bf16[448,3584]{1,0:T(8,128)(2,1)S(1)} %copy-done, f32[2048,448]{0,1:T(8,128)} %bitcast.174, f32[448]{0:T(512)S(1)} %copy-done.15, f32[2048]{0:T(1024)S(1)} %add_rsqrt_fusion, bf16[1,2048,448]{1,2,0:T(8,128)(2,1)} %param.12), kind=kOutput, calls=%fused_computation | convolution fusion | flops 6592266240 | bytes 23406336 | tf_op jit(solution)/shard_map/dot_general | solution.py:123
  164.5 0.7 copy-done.9
  165.2 0.1 convert_reduce_fusion
  165.3 0.2 fusion.54
  165.5 1.1 fusion.21
  166.6 0.2 broadcast_multiply_fusion
  166.8 0.7 fusion.12
  167.6 1.1 fusion.66
  168.7 2.1 convolution_add_fusion
  170.8 2.7 reshape.333
  173.5 3.4 copy.237
  176.9 3.3 reshape.334
  180.2 2.3 convolution_convert_fusion.1
  182.6 1.5 copy.148
  184.1 6.5 %all-to-all-start = ((bf16[16,7,4096]{2,1,0:T(8,128)(2,1)}), bf16[16,7,4096]{2,1,0:T(8,128)(2,1)}, u32[]{:S(2)}, u32[]{:S(2)}) async-start(bf16[16,7,4096]{2,1,0:T(8,128)(2,1)} %copy.148), calls=%async_computation.1 | async-start | bytes 2097152 | tf_op jit(solution)/shard_map/all_to_all | solution.py:136
  190.6 0.1 compare_reduce_fusion
  190.7 17.8 %all-to-all-done = bf16[16,7,4096]{2,1,0:T(8,128)(2,1)} async-done(((bf16[16,7,4096]{2,1,0:T(8,128)(2,1)}), bf16[16,7,4096]{2,1,0:T(8,128)(2,1)}, u32[]{:S(2)}, u32[]{:S(2)}) %all-to-all-start) | async-done | bytes 917536 | tf_op jit(solution)/shard_map/all_to_all | solution.py:136
  208.5 3.2 fusion.39
  211.7 142.2 %reduce-scatter.2.cloned.1.call-done = bf16[128,3584]{1,0:T(8,128)(2,1)} async-done(((bf16[2048,3584]{1,0:T(8,128)(2,1)}), bf16[128,3584]{1,0:T(8,128)(2,1)}) %reduce-scatter.2.cloned.1.call-update) | async-done | bytes 917520 | tf_op jit(solution)/shard_map/reduce_scatter | solution.py:122
  (47 shorter events, 0.4 us)
Async XLA Ops:
  7.2 142.1 %copy-start = (bf16[448,3584]{1,0:T(8,128)(2,1)S(1)}, bf16[448,3584]{1,0:T(8,128)(2,1)}, u32[]{:S(2)}) copy-start(bf16[448,3584]{1,0:T(8,128)(2,1)} %param.19) | copy-start | bytes 9633796
  7.2 14.7 %copy-start.8 = (f32[1,2048,7]{1,0,2:T(1,128)S(1)}, f32[1,2048,7]{1,0,2:T(1,128)}, u32[]{:S(2)}) copy-start(f32[1,2048,7]{1,0,2:T(1,128)} %param.15) | copy-start | bytes 172036
  7.2 346.7 %reduce-scatter.2.cloned.1.call-start = ((), (), s32[]{:S(2)}) async-start(), calls=%async_computation.2 | async-start | bytes 15597568 | tf_op jit(solution)/shard_map/reduce_scatter | solution.py:122
  13.3 0.6 copy-start.5
  26.6 3.8 %copy-start.7 = (f32[2048,7]{0,1:T(8,128)S(1)}, f32[2048,7]{0,1:T(8,128)}, u32[]{:S(2)}) copy-start(f32[2048,7]{0,1:T(8,128)} %reduce.3) | copy-start | bytes 172036
  26.6 3.8 %copy-start.10 = (f32[8,256]{1,0:T(8,128)S(1)}, f32[8,256]{1,0:T(8,128)}, u32[]{:S(2)}) copy-start(f32[8,256]{1,0:T(8,128)} %get-tuple-element.7) | copy-start | bytes 24580
  26.6 3.8 %copy-start.11 = (f32[8,256]{1,0:T(8,128)S(1)}, f32[8,256]{1,0:T(8,128)}, u32[]{:S(2)}) copy-start(f32[8,256]{1,0:T(8,128)} %get-tuple-element.8) | copy-start | bytes 24580
  26.6 3.9 %copy-start.1 = (bf16[56,8,8,256]{3,2,1,0:T(8,128)(2,1)S(1)}, bf16[56,8,8,256]{3,2,1,0:T(8,128)(2,1)}, u32[]{:S(2)}) copy-start(bf16[56,8,8,256]{3,2,1,0:T(8,128)(2,1)} %copy.177) | copy-start | bytes 5505028
  36.1 6.2 %copy-start.4 = (bf16[1,2048,448]{1,2,0:T(8,128)(2,1)S(1)}, bf16[1,2048,448]{1,2,0:T(8,128)(2,1)}, u32[]{:S(2)}) copy-start(bf16[1,2048,448]{1,2,0:T(8,128)(2,1)} %param.12) | copy-start | bytes 5505028
  45.1 0.7 copy-start.13
  45.1 2.5 copy-start.3
  47.7 0.7 copy-start.16
  53.2 96.1 %copy-start.15 = (f32[448]{0:T(512)S(1)}, f32[448]{0:T(512)}, u32[]{:S(2)}) copy-start(f32[448]{0:T(512)} %param.18) | copy-start | bytes 5380
  164.5 0.7 copy-start.9
  164.5 0.8 copy-start.6
  164.5 2.3 copy-start.2
  173.5 6.7 %copy-start.14 = (s32[8]{0:T(128)S(1)}, s32[8]{0:T(128)}, u32[]{:S(2)}) copy-start(s32[8]{0:T(128)} %get-tuple-element.11) | copy-start | bytes 100
  176.9 13.7 %copy-start.12 = (s32[16,8]{0,1:T(8,128)S(1)}, s32[16,8]{0,1:T(8,128)}, u32[]{:S(2)}) copy-start(s32[16,8]{0,1:T(8,128)} %param.21) | copy-start | bytes 1540
  184.1 24.4 %all-to-all-start = ((bf16[16,7,4096]{2,1,0:T(8,128)(2,1)}), bf16[16,7,4096]{2,1,0:T(8,128)(2,1)}, u32[]{:S(2)}, u32[]{:S(2)}) async-start(bf16[16,7,4096]{2,1,0:T(8,128)(2,1)} %copy.148), calls=%async_computation.1 | async-start | bytes 2097152 | tf_op jit(solution)/shard_map/all_to_all | solution.py:136
Sparse Core Ops, SparseCore 0:
  164.6 189.2 reduce-scatter.1
where the time goes:
time: 361 us
  waiting for transfers between devices  160 us (44%)
  blocking collectives  92.2 us (26%)
  matrix products  43.2 us (12%)
  local copies, waits for them, and re-layouts  30.9 us (9%)
  between operations  14.4 us (4%)
  other arithmetic  13.5 us (4%)
  starting transfers between devices  6.55 us (2%)
    reduce_scatter x1, waiting for transfers between devices, local(): lax.psum_scatter(jnp.dot(rounded, out_weight, preferred_element_type=jnp....  142 us
    psum x1, blocking collectives, local(): group_stat = lax.psum(sum_sq[:, None] * group_hot[None, :], 'tensor')  92.2 us
    all_to_all x1, waiting for transfers between devices, local(): lax.all_to_all(outbound.astype(jnp.bfloat16), 'dp', split_axis=0, concat_...  17.8 us
    dot_general x1, matrix products, local(): jnp.dot(rounded, out_weight, preferred_element_type=jnp.float32)  15.2 us
    unnamed x49, local copies, waits for them, and re-layouts  13 us
    dot_general x4, matrix products, split_einsum(): jnp.einsum(form, lower, narrow, preferred_element_type=jnp.float32)  11.7 us
    dot_general x4, matrix products, split_einsum(): first = jnp.einsum(form, upper, narrow, preferred_element_type=jnp.float32)  7.99 us
  transfers between devices with their start and end apart: 2, of which 2 were waited for; matrix products, arithmetic and copies ran while one was open for 6% of the time, Pallas kernels for 0%

commit v1 on v0

--- a/solution.py
+++ b/solution.py
@@ -1,3 +1,4 @@
+import functools
 import jax
 import jax.numpy as jnp
 from jax import lax
@@ -11,6 +12,14 @@
 BLOCK = 256
 INNER = 7168
 HIGHEST = lax.Precision.HIGHEST
+
+
+def arrange_stops_all(state, across):
+    low = lax.all_gather(state, across)
+    return jnp.sum(low, axis=0)
+
+
+_handle_panel = functools.partial(arrange_stops_all, across="tensor")
 
 
 def split_pair(values):
@@ -114,7 +123,7 @@
     gated = mixer_y * jax.nn.silu(gate_z[0].astype(jnp.float32))
     sum_sq = jnp.sum(gated * gated, axis=1)
     group_hot = (jnp.arange(NGROUPS) == group_idx).astype(jnp.float32)
-    group_stat = lax.psum(sum_sq[:, None] * group_hot[None, :], "tensor")
+    group_stat = _handle_panel(sum_sq[:, None] * group_hot[None, :])
     mean_sq = jnp.sum(group_stat * group_hot[None, :], axis=1) / (INNER // NGROUPS)
     rounded = (gated * lax.rsqrt(mean_sq + 1e-05)[:, None] * norm_gain[None, :]).astype(
         jnp.bfloat16

time: 361 us -> 304 us (0.84)
  blocking collectives: 92.2 us -> 35 us
    psum x1 -> x0, blocking collectives: 92.2 us -> none  [local(): group_stat = lax.psum(sum_sq[:, None] * group_hot[None, :], 'tensor')]
    reduce_scatter x1, waiting for transfers between devices: 142 us -> 72.6 us  [local(): lax.psum_scatter(jnp.dot(rounded, out_weight, preferred_element_type=jnp....]
    all_to_all x1, waiting for transfers between devices: 17.8 us -> 85.6 us  [local(): lax.all_to_all(outbound.astype(jnp.bfloat16), 'dp', split_axis=0, concat_...]
    all_gather x0 -> x1, blocking collectives: none -> 35 us  [arrange_stops_all(): low = lax.all_gather(state, across)]
  transfers between devices with their start and end apart: 2 -> 2, of which waited for: 2 -> 2; matrix products, arithmetic and copies ran while one was open for 6% -> 7% of each run, Pallas kernels for 0% -> 0%
where the time goes in v1:
time: 304 us; the launch traced here: 303 us
  waiting for transfers between devices  158 us (52%)
  matrix products  43.1 us (14%)
  blocking collectives  35 us (12%)
  local copies, waits for them, and re-layouts  30.9 us (10%)
  other arithmetic  14.6 us (5%)
  between operations  14.4 us (5%)
  starting transfers between devices  6.51 us (2%)
    all_to_all x1, waiting for transfers between devices, local(): lax.all_to_all(outbound.astype(jnp.bfloat16), 'dp', split_axis=0, concat_...  85.6 us
    reduce_scatter x1, waiting for transfers between devices, local(): lax.psum_scatter(jnp.dot(rounded, out_weight, preferred_element_type=jnp....  72.6 us
    all_gather x1, blocking collectives, arrange_stops_all(): low = lax.all_gather(state, across)  35 us
    dot_general x1, matrix products, local(): jnp.dot(rounded, out_weight, preferred_element_type=jnp.float32)  15.2 us
    unnamed x49, local copies, waits for them, and re-layouts  13 us
    dot_general x4, matrix products, split_einsum(): jnp.einsum(form, lower, narrow, preferred_element_type=jnp.float32)  11.7 us
    dot_general x4, matrix products, split_einsum(): first = jnp.einsum(form, upper, narrow, preferred_element_type=jnp.float32)  7.99 us
    all_to_all x1, starting transfers between devices, local(): lax.all_to_all(outbound.astype(jnp.bfloat16), 'dp', split_axis=0, concat_...  6.47 us
  transfers between devices with their start and end apart: 2, of which 2 were waited for; matrix products, arithmetic and copies ran while one was open for 7% of the time, Pallas kernels for 0%

profile of v1, /device:TPU:32, one launch (start us, length us, event | category | flops | bytes accessed | tf_op | source)
XLA Modules:
  0.0 302.9 jit_solution(5617816239584312320)
XLA Ops:
  7.2 0.5 broadcast.266
  7.8 1.4 reduce.9
  9.3 0.7 neg.22
  10.0 0.9 multiply_bitcast_fusion
  10.9 2.0 reduce-window.6
  12.9 0.2 slice_reduce_fusion
  13.1 0.2 reduce-window.9
  13.2 0.1 add_bitcast_fusion
  13.3 0.6 copy-done.5
  14.0 0.1 slice.37
  14.1 0.1 slice.38
  14.1 0.1 copy.200
  14.2 0.1 copy.199
  14.3 0.9 dynamic-slice_reduce_fusion
  15.2 0.6 and_select_fusion
  15.8 0.7 compare_convert_fusion
  16.5 0.7 fusion.58
  17.1 0.6 copy.272
  17.8 0.6 iota_compare_fusion
  18.4 3.3 %copy.208 = bf16[56,8,8,256]{3,2,1,0:T(8,128)(2,1)} copy(bf16[56,8,8,256]{3,1,2,0:T(8,128)(2,1)} %bitcast.168) | data formatting | bytes 3670016
  21.8 0.1 copy.201
  21.9 0.8 reduce.3
  22.7 0.1 copy.202
  22.8 2.5 constant_dynamic-slice_fusion
  25.3 1.2 copy.198
  26.7 1.0 copy.151
  27.6 1.3 compare_and_fusion
  28.9 1.5 fusion.46
  30.4 0.1 exponential_multiply_fusion
  30.5 5.6 %fusion.4 = f32[8,7,256,64]{2,3,1,0:T(8,128)S(1)} fusion(f32[8,256,256]{2,1,0:T(8,128)S(1)} %fusion.46, f32[8,7,256]{2,1,0:T(8,128)S(1)} %get-tuple-element.6, f32[8,7,256]{2,1,0:T(8,128)S(1)} %copy.151, pred[8,256,256]{2,1,0:T(8,128)(4,1)S(1)} %compare_and_fusion, bf16[8,256,7,64]{1,0,3,2:T(8,128)(2,1)S(1)} %bitcast.162), kind=kOutput, calls=%fused_computation.7 | convolution fusion | flops 488112128 | bytes 8241152 | tf_op jit(solution)/shard_map/bhts,bshp->bthp/dot_general | solution.py:33
  36.1 6.2 %fusion.1 = f32[8,7,256,64]{2,3,1,0:T(8,128)S(1)} fusion(f32[8,256,256]{2,1,0:T(8,128)S(1)} %fusion.46, f32[8,7,256]{2,1,0:T(8,128)S(1)} %get-tuple-element.6, f32[8,7,256]{2,1,0:T(8,128)S(1)} %copy.151, pred[8,256,256]{2,1,0:T(8,128)(4,1)S(1)} %compare_and_fusion, bf16[8,256,7,64]{1,0,3,2:T(8,128)(2,1)S(1)} %bitcast.163), kind=kOutput, calls=%fused_computation.5 | convolution fusion | flops 499122176 | bytes 8241152 | tf_op jit(solution)/shard_map/bhts,bshp->bthp/dot_general | solution.py:34
  42.3 0.4 convert_element_type.188
  42.8 1.7 copy.210
  44.5 0.7 fusion.23
  45.2 0.6 fusion.32
  45.8 0.1 select_exponential_fusion
  45.9 1.8 multiply_reduce_fusion
  47.7 0.6 fusion.44
  48.3 2.8 multiply_reduce_fusion.1
  51.1 2.1 copy.175
  53.2 3.7 %copy.209 = f32[56,8,8,256]{3,1,2,0:T(8,128)} copy(f32[56,8,8,256]{3,2,1,0:T(8,128)S(1)} %bitcast.160) | data formatting | bytes 7340032
  56.9 0.1 broadcast_multiply_fusion.1
  57.0 35.0 %all_gather.4 = f32[16,2048,2]{1,2,0:T(2,128)} all-gather(f32[1,2048,2]{1,2,0:T(2,128)S(1)} %broadcast_multiply_fusion.1), channel_id=1, replica_groups=mesh['dp'=16,'tensor'=16] {'tensor'}, dimensions={0}, use_global_device_ids=true | all-gather | bytes 278528 | tf_op jit(solution)/shard_map/all_gather | solution.py:18
  92.0 1.0 reduce_sum.47
  93.1 0.1 multiply_reduce_fusion.2
  93.2 15.2 %convolution_convert_fusion = bf16[2048,3584]{1,0:T(8,128)(2,1)} fusion(bf16[448,3584]{1,0:T(8,128)(2,1)S(1)} %copy-done, f32[2048,448]{0,1:T(8,128)} %bitcast.174, f32[448]{0:T(512)S(1)} %copy-done.15, f32[2048]{0:T(1024)S(1)} %add_rsqrt_fusion, bf16[1,2048,448]{1,2,0:T(8,128)(2,1)} %param.12), kind=kOutput, calls=%fused_computation | convolution fusion | flops 6592266240 | bytes 23406336 | tf_op jit(solution)/shard_map/dot_general | solution.py:132
  108.4 0.7 copy-done.9
  109.1 0.1 convert_reduce_fusion
  109.2 0.2 fusion.54
  109.4 1.1 fusion.21
  110.5 0.2 broadcast_multiply_fusion
  110.7 0.7 fusion.12
  111.5 1.1 fusion.66
  112.6 2.1 convolution_add_fusion
  114.7 2.7 reshape.385
  117.4 3.5 %copy.268 = f32[7,64,8,64]{3,1,0,2:T(8,128)} copy(f32[7,64,8,64]{3,2,1,0:T(8,128)} %reshape.385) | data formatting | bytes 1835008 | tf_op jit(solution)/shard_map/reshape | solution.py:119
  120.8 3.4 %reshape.386 = f32[8,28672]{1,0:T(8,128)} reshape(f32[8,7,64,64]{3,2,1,0:T(8,128)} %bitcast.167) | data formatting | bytes 1835008 | tf_op jit(solution)/shard_map/reshape | solution.py:121
  124.2 2.3 convolution_convert_fusion.1
  126.5 1.5 copy.179
  128.0 6.5 %all-to-all-start = ((bf16[16,7,4096]{2,1,0:T(8,128)(2,1)}), bf16[16,7,4096]{2,1,0:T(8,128)(2,1)}, u32[]{:S(2)}, u32[]{:S(2)}) async-start(bf16[16,7,4096]{2,1,0:T(8,128)(2,1)} %copy.179), calls=%async_computation.1 | async-start | bytes 2097152 | tf_op jit(solution)/shard_map/all_to_all | solution.py:145
  134.5 0.1 compare_reduce_fusion
  134.6 85.6 %all-to-all-done = bf16[16,7,4096]{2,1,0:T(8,128)(2,1)} async-done(((bf16[16,7,4096]{2,1,0:T(8,128)(2,1)}), bf16[16,7,4096]{2,1,0:T(8,128)(2,1)}, u32[]{:S(2)}, u32[]{:S(2)}) %all-to-all-start) | async-done | bytes 917536 | tf_op jit(solution)/shard_map/all_to_all | solution.py:145
  220.2 3.2 %fusion.39 = f32[8,7,4096]{2,0,1:T(8,128)} fusion(pred[16,8]{0,1:T(8,128)(4,1)S(1)} %compare_reduce_fusion, bf16[2,8,7,4096]{3,2,1,0:T(8,128)(2,1)} %bitcast.74), kind=kOutput, calls=%fused_computation.49 | convolution fusion | flops 7340032 | bytes 1835136 | tf_op jit(solution)/shard_map/dot_general | solution.py:150
  223.4 72.6 %reduce-scatter.2.cloned.1.call-done = bf16[128,3584]{1,0:T(8,128)(2,1)} async-done(((bf16[2048,3584]{1,0:T(8,128)(2,1)}), bf16[128,3584]{1,0:T(8,128)(2,1)}) %reduce-scatter.2.cloned.1.call-update) | async-done | bytes 917520 | tf_op jit(solution)/shard_map/reduce_scatter | solution.py:131
  (48 shorter events, 0.4 us)
Async XLA Ops:
  7.2 86.0 %copy-start = (bf16[448,3584]{1,0:T(8,128)(2,1)S(1)}, bf16[448,3584]{1,0:T(8,128)(2,1)}, u32[]{:S(2)}) copy-start(bf16[448,3584]{1,0:T(8,128)(2,1)} %param.19) | copy-start | bytes 9633796
  7.2 14.7 %copy-start.8 = (f32[1,2048,7]{1,0,2:T(1,128)S(1)}, f32[1,2048,7]{1,0,2:T(1,128)}, u32[]{:S(2)}) copy-start(f32[1,2048,7]{1,0,2:T(1,128)} %param.15) | copy-start | bytes 172036
  7.2 288.8 %reduce-scatter.2.cloned.1.call-start = ((), (), s32[]{:S(2)}) async-start(), calls=%async_computation.2 | async-start | bytes 15597568 | tf_op jit(solution)/shard_map/reduce_scatter | solution.py:131
  13.3 0.6 copy-start.5
  26.6 3.8 %copy-start.7 = (f32[2048,7]{0,1:T(8,128)S(1)}, f32[2048,7]{0,1:T(8,128)}, u32[]{:S(2)}) copy-start(f32[2048,7]{0,1:T(8,128)} %reduce.3) | copy-start | bytes 172036
  26.6 3.8 %copy-start.10 = (f32[8,256]{1,0:T(8,128)S(1)}, f32[8,256]{1,0:T(8,128)}, u32[]{:S(2)}) copy-start(f32[8,256]{1,0:T(8,128)} %get-tuple-element.7) | copy-start | bytes 24580
  26.6 3.8 %copy-start.11 = (f32[8,256]{1,0:T(8,128)S(1)}, f32[8,256]{1,0:T(8,128)}, u32[]{:S(2)}) copy-start(f32[8,256]{1,0:T(8,128)} %get-tuple-element.8) | copy-start | bytes 24580
  26.6 3.9 %copy-start.1 = (bf16[56,8,8,256]{3,2,1,0:T(8,128)(2,1)S(1)}, bf16[56,8,8,256]{3,2,1,0:T(8,128)(2,1)}, u32[]{:S(2)}) copy-start(bf16[56,8,8,256]{3,2,1,0:T(8,128)(2,1)} %copy.208) | copy-start | bytes 5505028
  36.1 6.2 %copy-start.4 = (bf16[1,2048,448]{1,2,0:T(8,128)(2,1)S(1)}, bf16[1,2048,448]{1,2,0:T(8,128)(2,1)}, u32[]{:S(2)}) copy-start(bf16[1,2048,448]{1,2,0:T(8,128)(2,1)} %param.12) | copy-start | bytes 5505028
  45.1 0.7 copy-start.13
  45.1 2.5 copy-start.3
  47.7 0.7 copy-start.16
  53.2 40.0 %copy-start.15 = (f32[448]{0:T(512)S(1)}, f32[448]{0:T(512)}, u32[]{:S(2)}) copy-start(f32[448]{0:T(512)} %param.18) | copy-start | bytes 5380
  108.4 0.7 copy-start.9
  108.4 0.8 copy-start.6
  108.4 2.3 copy-start.2
  117.4 6.8 %copy-start.14 = (s32[8]{0:T(128)S(1)}, s32[8]{0:T(128)}, u32[]{:S(2)}) copy-start(s32[8]{0:T(128)} %get-tuple-element.11) | copy-start | bytes 100
  120.8 13.6 %copy-start.12 = (s32[16,8]{0,1:T(8,128)S(1)}, s32[16,8]{0,1:T(8,128)}, u32[]{:S(2)}) copy-start(s32[16,8]{0,1:T(8,128)} %param.21) | copy-start | bytes 1540
  128.0 92.2 %all-to-all-start = ((bf16[16,7,4096]{2,1,0:T(8,128)(2,1)}), bf16[16,7,4096]{2,1,0:T(8,128)(2,1)}, u32[]{:S(2)}, u32[]{:S(2)}) async-start(bf16[16,7,4096]{2,1,0:T(8,128)(2,1)} %copy.179), calls=%async_computation.1 | async-start | bytes 2097152 | tf_op jit(solution)/shard_map/all_to_all | solution.py:145
Sparse Core Ops, SparseCore 0:
  108.5 187.4 reduce-scatter.1
